TPU v7x, 32 devices: a whole 2x2x4 slice. The times are simulated.
32 devices in a mesh: groups: 2 (over y), frame: 4 (over x, core), row: 4 (over z).
Axes of the slice: x: 2, y: 2, z: 4, core: 2. Of those that a mesh axis runs over, the one named last changes fastest.
Arguments:
- query_in: bfloat16 [8, 4, 64, 2240], P(('groups', 'frame'), 'row'), parts along dimension 0, may hold values from -6 to 6
- key_in: bfloat16 [8, 4, 64, 2240], P(('groups', 'frame'), 'row'), parts along dimension 0, may hold values from -216 to 216
- value_in: bfloat16 [8, 4, 64, 2240], P(('groups', 'frame'), 'row'), parts along dimension 0, may hold values from -6 to 6
- stream_in: bfloat16 [8, 4, 64, 2240], P(('groups', 'frame'), 'row'), parts along dimension 0, may hold values from -6 to 6
- attn_gain: bfloat16 [2240], replicated, may hold values from 0.5 to 1.5
- ffn_gain: bfloat16 [2240], replicated, may hold values from 0.5 to 1.5
- in_weight: bfloat16 [2240, 2, 3360], P('row', None, 'frame'), may hold values from -0.125 to 0.125
- conv_weight: bfloat16 [9, 2, 3360], P(None, None, 'frame'), may hold values from -3.5 to 3.5
- out_weight: bfloat16 [3360, 2240], P('frame'), may hold values from -0.109375 to 0.109375
Outputs:
- stream_out: bfloat16 [8, 4, 64, 2240], P(('groups', 'frame'), 'row'), parts along dimension 0
- block_out: bfloat16 [8, 4, 64, 2240], P(('groups', 'frame'), 'row'), parts along dimension 0
There are 2 independent parts, one for each index of `groups`. A program takes and returns all parts, laid end to end along the dimension named above; an argument that names none is the same for every part. Nothing has to cross between parts.
All inputs are finite; a program needn't handle non-finite values.
Results may differ from a plain program's by a relative error of at most 0.01.
Values may be sent and summed in bfloat16 or wider, within the bound.
No kernel may reach another device: no remote copies, remote signals or barrier semaphores. Data moves between devices by JAX's collectives and lax.ppermute only.
A program may use at most 64 MiB of HBM per device.

v0:
```python
import jax
import jax.numpy as jnp
from jax import lax
from jax.sharding import PartitionSpec as P

HEADS = 20
HEAD_DIM = 112
NORM_EPS = 1e-06
SHARE_EPS = 1e-06


def padded_2(cells, sides, width):
    for axis, dim in sides:
        count = lax.axis_size(axis)
        ends = count - 1
        head = lax.slice_in_dim(cells, 0, width, axis=dim)
        tail = lax.slice_in_dim(cells, cells.shape[dim] - width, cells.shape[dim], axis=dim)
        cells = jnp.concatenate(
            [
                lax.ppermute(tail, axis, [(i, (i + 1) % count) for i in range(ends)]),
                cells,
                lax.ppermute(head, axis, [((i + 1) % count, i) for i in range(ends)]),
            ],
            axis=dim,
        )
    return cells


def rms_norm(features):
    return features * lax.rsqrt(jnp.mean(features * features, axis=-1, keepdims=True) + NORM_EPS)


def depthwise(padded, conv_taps, row_count, col_count, half_width):
    widened = jnp.pad(padded, ((0, 0), (0, 0), (1, 1), (0, 0)))
    summed = jnp.zeros((padded.shape[0], row_count, col_count, padded.shape[3]), jnp.float32)
    for row_off in range(3):
        for col_off in range(3):
            window = widened[
                :, row_off : row_off + row_count, col_off : col_off + col_count, :
            ].astype(jnp.float32)
            summed = summed + window * conv_taps[row_off * 3 + col_off]
    return (summed[..., :half_width] * jax.nn.silu(summed[..., half_width:])).astype(jnp.bfloat16)


def local(
    query_in, key_in, value_in, stream_in, attn_gain, ffn_gain, in_weight, conv_weight, out_weight
):
    frame_count, row_count, col_count, model_width = query_in.shape
    token_count = frame_count * row_count * col_count
    local_gated = in_weight.shape[2]
    highest = lax.Precision.HIGHEST
    key_pos = jnp.maximum(key_in, 0).reshape(token_count, HEADS, HEAD_DIM)
    value_heads = value_in.reshape(token_count, HEADS, HEAD_DIM)
    local_state = jnp.einsum(
        "thi,thj->ihj", key_pos, value_heads, preferred_element_type=jnp.float32
    ).reshape(HEAD_DIM, model_width)
    local_total = jnp.sum(key_pos.reshape(token_count, model_width), axis=0, dtype=jnp.float32)
    state_share, total_share = (
        lax.psum_scatter(
            local_state.astype(jnp.bfloat16), "row", scatter_dimension=1, tiled=True
        ).astype(jnp.float32),
        lax.psum_scatter(
            local_total.astype(jnp.bfloat16), "row", scatter_dimension=0, tiled=True
        ).astype(jnp.float32),
    )
    state_share, total_share = lax.psum((state_share, total_share), "frame")
    kv_state, key_total = (
        lax.all_gather(state_share, "row", axis=1, tiled=True),
        lax.all_gather(total_share, "row", axis=0, tiled=True),
    )
    query_pos = jnp.maximum(query_in, 0).reshape(token_count, HEADS, HEAD_DIM).astype(jnp.float32)
    numerator = jnp.einsum(
        "thi,ihj->thj", query_pos, kv_state.reshape(HEAD_DIM, HEADS, HEAD_DIM), precision=highest
    )
    denominator = jnp.einsum(
        "thi,hi->th", query_pos, key_total.reshape(HEADS, HEAD_DIM), precision=highest
    )
    attended = (numerator / (denominator[:, :, None] + SHARE_EPS)).reshape(token_count, model_width)
    stream_flat = stream_in.reshape(token_count, model_width).astype(jnp.float32)
    stream_out = (stream_flat + attn_gain.astype(jnp.float32) * rms_norm(attended)).astype(
        jnp.bfloat16
    )
    normed = (rms_norm(stream_out.astype(jnp.float32)) * ffn_gain.astype(jnp.float32)).astype(
        jnp.bfloat16
    )
    normed_grid = normed.reshape(frame_count, row_count, col_count, model_width)
    in_full = lax.all_gather(in_weight, "row", axis=0, tiled=True).reshape(
        model_width, 2 * local_gated
    )
    conv_taps = conv_weight.reshape(9, 2 * local_gated).astype(jnp.float32)
    frame_piece = lax.all_gather(normed_grid, "frame", axis=0, tiled=True)
    piece_frames = frame_piece.shape[0]
    piece_rows = frame_piece.shape[1]
    projected = jnp.dot(
        frame_piece.reshape(piece_frames * piece_rows * col_count, model_width),
        in_full,
        preferred_element_type=jnp.float32,
    )
    expanded = (
        jax.nn.silu(projected)
        .astype(jnp.bfloat16)
        .reshape(piece_frames, piece_rows, col_count, 2 * local_gated)
    )
    padded_expanded = padded_2(expanded, (("row", 1),), 1)
    hidden = depthwise(padded_expanded, conv_taps, row_count, col_count, local_gated)
    hidden_flat = hidden.reshape(-1, local_gated)
    ffn_rows = lax.psum_scatter(
        jnp.dot(hidden_flat, out_weight, preferred_element_type=jnp.float32).astype(jnp.bfloat16),
        "frame",
        scatter_dimension=0,
        tiled=True,
    ).astype(jnp.float32)
    block_out = (stream_out.astype(jnp.float32) + ffn_rows).astype(jnp.bfloat16)
    grid_shape = (frame_count, row_count, col_count, model_width)
    return (stream_out.reshape(grid_shape), block_out.reshape(grid_shape))


def solution(mesh):
    in_specs = (
        P(("groups", "frame"), "row", None, None),
        P(("groups", "frame"), "row", None, None),
        P(("groups", "frame"), "row", None, None),
        P(("groups", "frame"), "row", None, None),
        P(),
        P(),
        P("row", None, "frame"),
        P(None, None, "frame"),
        P("frame", None),
    )
    out_specs = (
        P(("groups", "frame"), "row", None, None),
        P(("groups", "frame"), "row", None, None),
    )
    return jax.shard_map(local, mesh=mesh, in_specs=in_specs, out_specs=out_specs, check_vma=False)
```

profile of v0, /device:TPU:0, one launch (start us, length us, event | category | flops | bytes accessed | tf_op | source)
XLA Modules:
  0.0 293.6 jit_solution(11495132540162727477)
XLA Ops:
  7.2 0.0 reduce-scatter.3.cloned.1.call-start
  7.2 1.1 fusion.21
  8.3 0.4 reshape.204
  8.7 1.4 reshape.205
  10.1 0.4 fusion.7
  10.4 0.0 copy-start.3
  10.5 0.0 copy-start.4
  10.5 0.0 copy-start.1
  10.5 1.1 copy.25
  11.6 0.0 reduce-scatter.3.cloned.1.call-update
  11.6 0.0 all-gather.5.cloned.1.call-start
  11.6 0.7 all-gather.5.cloned.1.call-update
  12.4 0.0 all-gather.3.cloned.1.call-start
  12.4 0.0 copy-done.3
  12.4 0.0 copy-done.4
  12.5 0.0 copy-done.1
  12.5 0.4 reshape.207
  12.9 0.0 copy-done.5
  12.9 0.6 fusion.25
  14.8 14.3 %all-reduce.2 = bf16[2240]{0:T(1024)(128)(2,1)S(1)} all-reduce(bf16[2240]{0:T(1024)(128)(2,1)S(1)} %get-tuple-element.8), channel_id=3, replica_groups=mesh['groups'=2,'frame'=4,'row'=4] {'row'}, use_global_device_ids=true, to_apply=%region_3.0.clone | all-reduce | flops 2240 | bytes 8960
  29.2 0.1 dynamic-slice_convert_fusion
  29.3 7.2 %reduce-scatter.3.cloned.1.call-done = bf16[112,560]{0,1:T(8,128)(2,1)} async-done(((bf16[112,2240]{0,1:T(8,128)(2,1)}), bf16[112,560]{0,1:T(8,128)(2,1)}) %reduce-scatter.3.cloned.1.call-update) | async-done | bytes 125456 | tf_op jit(solution)/shard_map/reduce_scatter | solution.py:59
  36.5 13.6 %all-reduce.5 = (f32[112,560]{0,1:T(8,128)S(1)}, f32[560]{0:T(1024)S(1)}) all-reduce(bf16[112,560]{0,1:T(8,128)(2,1)} %reduce-scatter.3.cloned.1.call-done, f32[560]{0:T(1024)S(1)} %dynamic-slice_convert_fusion), channel_id=1, replica_groups=mesh['groups'=2,'frame'=4,'row'=4] {'frame'}, use_global_device_ids=true, to_apply=%region_1.0 | all-reduce | flops 63280 | bytes 380800 | tf_op jit(solution)/shard_map/psum | solution.py:66
  50.1 0.3 dynamic-update-slice
  50.4 19.7 %all-reduce.1 = f32[2240]{0:T(1024)S(1)} all-reduce(f32[2240]{0:T(1024)S(1)} %dynamic-update-slice), channel_id=1, replica_groups=mesh['groups'=2,'frame'=4,'row'=4] {'row'}, use_global_device_ids=true, to_apply=%add.1 | all-reduce | flops 2240 | bytes 17920
  70.1 0.1 reshape.225
  70.2 0.6 fusion.17
  70.8 42.0 %all_gather.12 = f32[112,2240]{0,1:T(8,128)S(1)} all-gather(f32[112,560]{0,1:T(8,128)S(1)} %get-tuple-element.2), channel_id=1, replica_groups=mesh['groups'=2,'frame'=4,'row'=4] {'row'}, dimensions={1}, use_global_device_ids=true | all-gather | bytes 1254400 | tf_op jit(solution)/shard_map/all_gather | solution.py:68
  112.8 1.4 multiply_reduce_fusion
  114.2 0.0 copy-start
  114.2 0.4 copy.28
  114.6 0.2 reshape.210
  114.8 0.2 reshape.209
  115.1 0.1 copy-done
  115.1 0.3 fusion.12
  115.4 1.0 multiply_convert_fusion.1
  116.5 0.0 all-gather.3.cloned.1.call-update
  116.5 0.0 reduce-scatter.5.cloned.1.call-start
  116.6 82.5 %all-gather.5.cloned.1.call-done = bf16[2240,2,840]{2,1,0:T(2,128)(2,1)} async-done(((bf16[560,2,840]{2,1,0:T(2,128)(2,1)}), bf16[2240,2,840]{2,1,0:T(2,128)(2,1)}) %all-gather.5.cloned.1.call-update) | async-done | bytes 7526416 | tf_op jit(solution)/shard_map/all_gather | solution.py:87
  199.1 22.9 %copy.30 = bf16[2240,2,840]{0,2,1:T(8,128)(2,1)} copy(bf16[2240,2,840]{2,1,0:T(2,128)(2,1)} %all-gather.5.cloned.1.call-done) | data formatting | bytes 15052800 | tf_op jit(solution)/shard_map/all_gather | solution.py:87
  221.9 5.8 %multiply_convert_fusion = bf16[256,1680]{0,1:T(8,128)(2,1)S(1)} fusion(bf16[256,2240]{1,0:T(8,128)(2,1)} %bitcast.49, bf16[2240,1680]{0,1:T(8,128)(2,1)} %bitcast.45), kind=kOutput, calls=%fused_computation.10 | convolution fusion | flops 1928908800 | bytes 9533440 | tf_op jit(solution)/shard_map/dot_general | solution.py:94
  227.8 0.6 copy.31
  228.4 1.3 collective-permute-start.1
  229.7 4.8 %collective-permute-start = (bf16[4,1,64,1680]{3,2,0,1:T(8,128)(2,1)S(1)}, bf16[4,1,64,1680]{3,2,0,1:T(8,128)(2,1)S(1)}, u32[]{:S(2)}, u32[]{:S(2)}) collective-permute-start(bf16[4,1,64,1680]{3,2,0,1:T(8,128)(2,1)S(1)} %bitcast.42), channel_id=1, source_target_pairs={{0,1},{1,2},{2,3},{4,5},{5,6},{6,7},{8,9},{9,10},{10,11},{12,13},{... | collective-permute-start | bytes 2580488 | tf_op jit(solution)/shard_map/ppermute | solution.py:20
  234.5 0.0 copy-done.2
  234.5 0.1 mul.187
  234.6 0.1 mul.190
  234.7 0.1 mul.193
  234.8 0.1 mul.196
  234.8 0.1 mul.199
  234.9 0.1 mul.202
  235.0 0.1 mul.205
  235.1 0.1 mul.208
  235.2 0.1 mul.211
  235.2 17.3 %collective-permute-done.1 = bf16[4,1,64,1680]{3,2,0,1:T(8,128)(2,1)S(1)} collective-permute-done((bf16[4,1,64,1680]{3,2,0,1:T(8,128)(2,1)S(1)}, bf16[4,1,64,1680]{3,2,0,1:T(8,128)(2,1)S(1)}, u32[]{:S(2)}, u32[]{:S(2)}) %collective-permute-start.1) | collective-permute-done | bytes 860192 | tf_op jit(solution)/shard_map/ppermute | solution.py:22
  252.6 1.2 collective-permute-done
  253.8 1.1 fusion.5
  254.8 0.0 copy-start.6
  254.9 1.8 multiply_add_fusion
  256.6 0.3 fusion.8
  257.0 2.4 convolution_convert_fusion
  259.4 0.0 reduce-scatter.5.cloned.1.call-update
  259.4 26.0 %reduce-scatter.5.cloned.1.call-done = bf16[64,2240]{1,0:T(8,128)(2,1)} async-done(((bf16[256,2240]{1,0:T(8,128)(2,1)}), bf16[64,2240]{1,0:T(8,128)(2,1)}) %reduce-scatter.5.cloned.1.call-update) | async-done | bytes 286736 | tf_op jit(solution)/shard_map/reduce_scatter | solution.py:107
  285.4 1.7 fusion.16
  (12 shorter events, 0.1 us)
Async XLA Ops:
  7.2 29.3 %reduce-scatter.3.cloned.1.call-start = ((), (), s32[]{:S(2)}) async-start(), calls=%async_computation.2 | async-start | bytes 716800 | tf_op jit(solution)/shard_map/reduce_scatter | solution.py:59
  10.4 2.0 copy-start.3
  10.5 2.0 copy-start.4
  10.5 2.0 copy-start.1
  11.6 1.4 copy-start.5
  11.6 187.5 %all-gather.5.cloned.1.call-start = ((), (), s32[]{:S(2)}) async-start(), calls=%async_computation.4 | async-start | bytes 10035200 | tf_op jit(solution)/shard_map/all_gather | solution.py:87
  12.4 209.6 %all-gather.3.cloned.1.call-start = ((), (), s32[]{:S(2)}) async-start(), calls=%async_computation.3 | async-start | bytes 1474560 | tf_op jit(solution)/shard_map/all_gather | solution.py:91
  114.2 1.0 copy-start
  116.5 168.9 %reduce-scatter.5.cloned.1.call-start = ((), (), s32[]{:S(2)}) async-start(), calls=%async_computation.5 | async-start | bytes 1474560 | tf_op jit(solution)/shard_map/reduce_scatter | solution.py:107
  221.9 12.6 %copy-start.2 = (bf16[9,2,840]{2,1,0:T(2,128)(2,1)S(1)}, bf16[9,2,840]{2,1,0:T(2,128)(2,1)}, u32[]{:S(2)}) copy-start(bf16[9,2,840]{2,1,0:T(2,128)(2,1)} %param.16) | copy-start | bytes 90724
  228.4 24.2 %collective-permute-start.1 = (bf16[4,1,64,1680]{3,2,0,1:T(8,128)(2,1)S(1)}, bf16[4,1,64,1680]{3,2,0,1:T(8,128)(2,1)S(1)}, u32[]{:S(2)}, u32[]{:S(2)}) collective-permute-start(bf16[4,1,64,1680]{3,2,0,1:T(8,128)(2,1)S(1)} %bitcast.41), channel_id=1, source_target_pairs={{1,0},{2,1},{3,2},{5,4},{6,5},{7,6},{9,8},{10,9},{11,10},{13,12},{... | collective-permute-start | bytes 2580488 | tf_op jit(solution)/shard_map/ppermute | solution.py:22
  229.7 24.1 %collective-permute-start = (bf16[4,1,64,1680]{3,2,0,1:T(8,128)(2,1)S(1)}, bf16[4,1,64,1680]{3,2,0,1:T(8,128)(2,1)S(1)}, u32[]{:S(2)}, u32[]{:S(2)}) collective-permute-start(bf16[4,1,64,1680]{3,2,0,1:T(8,128)(2,1)S(1)} %bitcast.42), channel_id=1, source_target_pairs={{0,1},{1,2},{2,3},{4,5},{5,6},{6,7},{8,9},{9,10},{10,11},{12,13},{... | collective-permute-start | bytes 2580488 | tf_op jit(solution)/shard_map/ppermute | solution.py:20
  254.8 2.1 copy-start.6
Sparse Core Ops, SparseCore 0:
  11.7 24.6 reduce-scatter.2
  38.0 160.9 all-gather.4
  201.2 15.6 all-gather.2
  259.5 25.7 reduce-scatter.4
where the time goes:
time: 295 us; the launch traced here: 294 us
  waiting for transfers between devices  135 us (46%)
  blocking collectives  89.6 us (30%)
  local copies, waits for them, and re-layouts  29.5 us (10%)
  between operations  15.4 us (5%)
  matrix products  10.6 us (4%)
  other arithmetic  7.42 us (3%)
  starting transfers between devices  6.24 us (2%)
    all_gather x1, waiting for transfers between devices, local(): lax.all_gather(in_weight, 'row', axis=0, tiled=True)  82.5 us
    all_gather x1, blocking collectives, local(): lax.all_gather(state_share, 'row', axis=1, tiled=True)  42 us
    unnamed x2, blocking collectives  34 us
    reduce_scatter x1, waiting for transfers between devices, local(): lax.psum_scatter(jnp.dot(hidden_flat, out_weight, preferred_element_type=...  26 us
    all_gather x1, local copies, waits for them, and re-layouts, local(): lax.all_gather(in_weight, 'row', axis=0, tiled=True)  22.9 us
    ppermute x1, waiting for transfers between devices, padded_2(): lax.ppermute(head, axis, [((i + 1) % count, i) for i in range(ends)])  17.3 us
    psum x1, blocking collectives, local(): state_share, total_share = lax.psum((state_share, total_share), 'frame')  13.6 us
    reduce_scatter x1, waiting for transfers between devices, local(): lax.psum_scatter(local_state.astype(jnp.bfloat16), 'row', scatter_dimensi...  7.19 us
  transfers between devices with their start and end apart: 6, of which 5 were waited for; matrix products, arithmetic and copies ran while one was open for 10% of the time, Pallas kernels for 0%

commit v1 on v0

--- a/solution.py
+++ b/solution.py
@@ -7,6 +7,24 @@
 HEAD_DIM = 112
 NORM_EPS = 1e-06
 SHARE_EPS = 1e-06
+
+
+def gather_around(value, axis, dim):
+    ways, here, step = (lax.axis_size(axis), lax.axis_index(axis), value.shape[dim])
+    shape = [n * ways if d == dim else n for d, n in enumerate(value.shape)]
+    full = lax.dynamic_update_slice_in_dim(
+        jnp.zeros(shape, value.dtype), value, here * step, axis=dim
+    )
+    going_up = going_down = value
+    for far in range(1, ways // 2 + 1):
+        going_up = lax.ppermute(going_up, axis, [(d, (d + 1) % ways) for d in range(ways)])
+        full = lax.dynamic_update_slice_in_dim(full, going_up, (here - far) % ways * step, axis=dim)
+        if 2 * far < ways:
+            going_down = lax.ppermute(going_down, axis, [(d, (d - 1) % ways) for d in range(ways)])
+            full = lax.dynamic_update_slice_in_dim(
+                full, going_down, (here + far) % ways * step, axis=dim
+            )
+    return full
 
 
 def padded_2(cells, sides, width):
@@ -84,9 +102,7 @@
         jnp.bfloat16
     )
     normed_grid = normed.reshape(frame_count, row_count, col_count, model_width)
-    in_full = lax.all_gather(in_weight, "row", axis=0, tiled=True).reshape(
-        model_width, 2 * local_gated
-    )
+    in_full = gather_around(in_weight, "row", 0).reshape(model_width, 2 * local_gated)
     conv_taps = conv_weight.reshape(9, 2 * local_gated).astype(jnp.float32)
     frame_piece = lax.all_gather(normed_grid, "frame", axis=0, tiled=True)
     piece_frames = frame_piece.shape[0]

time: 295 us -> 355 us (1.20)
  waiting for transfers between devices: 135 us -> 41.9 us
  local copies, waits for them, and re-layouts: 29.5 us -> 118 us
  blocking collectives: 89.6 us -> 148 us
  starting transfers between devices: 6.24 us -> 10.2 us
    dynamic_update_slice x0 -> x4, local copies, waits for them, and re-layouts: none -> 90.5 us  [the longest x2 45.9 us: gather_around(): lax.dynamic_update_slice_in_dim(full, going_up, (here - far) % ways * ste...]
    all_gather x1 -> x0, waiting for transfers between devices: 82.5 us -> none  [local(): lax.all_gather(in_weight, 'row', axis=0, tiled=True)]
    unnamed x2, blocking collectives: 34 us -> 113 us
    all_gather x1 -> x0, local copies, waits for them, and re-layouts: 22.9 us -> none  [local(): lax.all_gather(in_weight, 'row', axis=0, tiled=True)]
    all_gather x1, blocking collectives: 42 us -> 20.6 us  [local(): lax.all_gather(state_share, 'row', axis=1, tiled=True)]
    ppermute x1, waiting for transfers between devices: 17.3 us -> 5.5 us  [padded_2(): lax.ppermute(head, axis, [((i + 1) % count, i) for i in range(ends)])]
    ppermute x1, waiting for transfers between devices: 1.18 us -> 12.1 us  [padded_2(): lax.ppermute(tail, axis, [(i, (i + 1) % count) for i in range(ends)])]
    ppermute x0 -> x3, local copies, waits for them, and re-layouts: none -> 10.6 us  [the longest x2 7.09 us: gather_around(): lax.ppermute(going_up, axis, [(d, (d + 1) % ways) for d in range(ways)])]
  transfers between devices with their start and end apart: 6 -> 8, of which waited for: 5 -> 3; matrix products, arithmetic and copies ran while one was open for 10% -> 33% of each run, Pallas kernels for 0% -> 0%
where the time goes in v1:
time: 355 us; the launch traced here: 351 us
  blocking collectives  148 us (42%)
  local copies, waits for them, and re-layouts  118 us (33%)
  waiting for transfers between devices  41.9 us (12%)
  between operations  15.4 us (4%)
  matrix products  10.6 us (3%)
  starting transfers between devices  10.2 us (3%)
  other arithmetic  7.45 us (2%)
    unnamed x2, blocking collectives  113 us
    dynamic_update_slice x2, local copies, waits for them, and re-layouts, gather_around(): lax.dynamic_update_slice_in_dim(full, going_up, (here - far) % ways * ste...  45.9 us
    reduce_scatter x1, waiting for transfers between devices, local(): lax.psum_scatter(jnp.dot(hidden_flat, out_weight, preferred_element_type=...  24.3 us
    dynamic_update_slice x1, local copies, waits for them, and re-layouts, gather_around(): lax.dynamic_update_slice_in_dim(full, going_down, (here + far) % ways * s...  23.5 us
    dynamic_update_slice x1, local copies, waits for them, and re-layouts, gather_around(): lax.dynamic_update_slice_in_dim(jnp.zeros(shape, value.dtype), value, her...  21.1 us
    all_gather x1, blocking collectives, local(): lax.all_gather(state_share, 'row', axis=1, tiled=True)  20.6 us
    psum x1, blocking collectives, local(): state_share, total_share = lax.psum((state_share, total_share), 'frame')  13.8 us
    ppermute x1, waiting for transfers between devices, padded_2(): lax.ppermute(tail, axis, [(i, (i + 1) % count) for i in range(ends)])  12.1 us
  transfers between devices with their start and end apart: 8, of which 3 were waited for; matrix products, arithmetic and copies ran while one was open for 33% of the time, Pallas kernels for 0%

profile of v1, /device:TPU:0, one launch (start us, length us, event | category | flops | bytes accessed | tf_op | source)
XLA Modules:
  0.0 351.5 jit_solution(9925255957794126768)
XLA Ops:
  7.2 0.0 reduce-scatter.3.cloned.1.call-start
  7.2 1.1 fusion.21
  8.3 0.4 reshape.204
  8.7 1.5 reshape.205
  10.2 0.4 fusion.7
  10.6 1.1 copy.27
  11.7 0.0 reduce-scatter.3.cloned.1.call-update
  11.7 0.0 copy-start.2
  11.8 0.0 copy-start.6
  11.8 0.0 all-gather.2.cloned.1.call-start
  11.8 1.5 copy.33
  13.4 3.0 collective-permute-start
  16.4 2.0 collective-permute-start.1
  18.5 0.4 reshape.207
  18.9 0.6 fusion.25
  20.8 97.5 %all-reduce.2 = bf16[2240]{0:T(1024)(128)(2,1)S(1)} all-reduce(bf16[2240]{0:T(1024)(128)(2,1)S(1)} %get-tuple-element.8), channel_id=3, replica_groups=mesh['groups'=2,'frame'=4,'row'=4] {'row'}, use_global_device_ids=true, to_apply=%region_3.0.clone | all-reduce | flops 2240 | bytes 8960
  118.4 0.1 dynamic-slice_convert_fusion
  118.5 13.8 %all-reduce.5 = (f32[112,560]{0,1:T(8,128)S(1)}, f32[560]{0:T(1024)S(1)}) all-reduce(bf16[112,560]{0,1:T(8,128)(2,1)} %reduce-scatter.3.cloned.1.call-done, f32[560]{0:T(1024)S(1)} %dynamic-slice_convert_fusion), channel_id=1, replica_groups=mesh['groups'=2,'frame'=4,'row'=4] {'frame'}, use_global_device_ids=true, to_apply=%region_1.0 | all-reduce | flops 63280 | bytes 380800 | tf_op jit(solution)/shard_map/psum | solution.py:84
  132.3 0.3 dynamic-update-slice
  132.6 15.8 %all-reduce.1 = f32[2240]{0:T(1024)S(1)} all-reduce(f32[2240]{0:T(1024)S(1)} %dynamic-update-slice), channel_id=1, replica_groups=mesh['groups'=2,'frame'=4,'row'=4] {'row'}, use_global_device_ids=true, to_apply=%add.1 | all-reduce | flops 2240 | bytes 17920
  148.4 0.1 reshape.225
  148.5 0.6 fusion.17
  149.1 20.6 %all_gather.9 = f32[112,2240]{0,1:T(8,128)S(1)} all-gather(f32[112,560]{0,1:T(8,128)S(1)} %get-tuple-element.2), channel_id=1, replica_groups=mesh['groups'=2,'frame'=4,'row'=4] {'row'}, dimensions={1}, use_global_device_ids=true | all-gather | bytes 1254400 | tf_op jit(solution)/shard_map/all_gather | solution.py:86
  169.7 1.4 multiply_reduce_fusion
  171.1 0.4 copy.30
  171.5 0.2 reshape.210
  171.8 0.2 reshape.209
  172.0 0.1 copy-done.1
  172.1 0.3 fusion.12
  172.4 0.1 collective-permute-start.2
  172.6 1.0 multiply_convert_fusion.1
  173.6 0.0 all-gather.2.cloned.1.call-update
  173.6 0.2 reduce-scatter.5.cloned.1.call-start
  173.9 5.0 %copy.32 = bf16[560,2,840]{0,2,1:T(8,128)(2,1)S(1)} copy(bf16[560,2,840]{2,1,0:T(2,128)(2,1)} %param.15) | data formatting | bytes 3763200 | tf_op args[6]
  178.9 3.7 %broadcast_in_dim.2 = bf16[2240,2,840]{0,2,1:T(8,128)(2,1)} broadcast(bf16[]{:T(256)} %constant.42.clone.1), dimensions={} | broadcast | bytes 7526402 | tf_op jit(solution)/shard_map/broadcast_in_dim | solution.py:16
  182.5 21.1 %dynamic_update_slice.12 = bf16[2240,2,840]{0,2,1:T(8,128)(2,1)} dynamic-update-slice(bf16[2240,2,840]{0,2,1:T(8,128)(2,1)} %broadcast_in_dim.2, bf16[560,2,840]{0,2,1:T(8,128)(2,1)S(1)} %copy.32, s32[]{:T(128)S(6)} %select_n.27, s32[]{:T(128)} %constant.48.clone.1, s32[]{:T(128)} %constant.48.clone.1) | dynamic-update-slice | bytes 3763204 | tf_op jit(solution)/shard_map/dynamic_update_slice | solution.py:15
  203.7 3.5 %copy.34 = bf16[560,2,840]{0,2,1:T(8,128)(2,1)S(1)} copy(bf16[560,2,840]{2,0,1:T(8,128)(2,1)} %collective-permute-done) | data formatting | bytes 3763200 | tf_op jit(solution)/shard_map/ppermute | solution.py:20
  207.2 22.4 %dynamic_update_slice.13 = bf16[2240,2,840]{0,2,1:T(8,128)(2,1)} dynamic-update-slice(bf16[2240,2,840]{0,2,1:T(8,128)(2,1)} %dynamic_update_slice.12, bf16[560,2,840]{0,2,1:T(8,128)(2,1)S(1)} %copy.34, s32[]{:T(128)S(6)} %select_n.29, s32[]{:T(128)} %constant.48.clone.1, s32[]{:T(128)} %constant.48.clone.1) | dynamic-update-slice | bytes 3763204 | tf_op jit(solution)/shard_map/dynamic_update_slice | solution.py:21
  229.6 3.5 %copy.36 = bf16[560,2,840]{0,2,1:T(8,128)(2,1)S(1)} copy(bf16[560,2,840]{2,0,1:T(8,128)(2,1)} %collective-permute-done.1) | data formatting | bytes 3763200 | tf_op jit(solution)/shard_map/ppermute | solution.py:23
  233.2 23.5 %dynamic_update_slice.14 = bf16[2240,2,840]{0,2,1:T(8,128)(2,1)} dynamic-update-slice(bf16[2240,2,840]{0,2,1:T(8,128)(2,1)} %dynamic_update_slice.13, bf16[560,2,840]{0,2,1:T(8,128)(2,1)S(1)} %copy.36, s32[]{:T(128)S(6)} %select_n.31, s32[]{:T(128)} %constant.48.clone.1, s32[]{:T(128)} %constant.48.clone.1) | dynamic-update-slice | bytes 3763204 | tf_op jit(solution)/shard_map/dynamic_update_slice | solution.py:24
  256.7 3.5 %copy.37 = bf16[560,2,840]{0,2,1:T(8,128)(2,1)S(1)} copy(bf16[560,2,840]{2,0,1:T(8,128)(2,1)} %collective-permute-done.2) | data formatting | bytes 3763200 | tf_op jit(solution)/shard_map/ppermute | solution.py:20
  260.2 23.5 %dynamic_update_slice.15 = bf16[2240,2,840]{0,2,1:T(8,128)(2,1)} dynamic-update-slice(bf16[2240,2,840]{0,2,1:T(8,128)(2,1)} %dynamic_update_slice.14, bf16[560,2,840]{0,2,1:T(8,128)(2,1)S(1)} %copy.37, s32[]{:T(128)S(6)} %select_n.33, s32[]{:T(128)} %constant.48.clone.1, s32[]{:T(128)} %constant.48.clone.1) | dynamic-update-slice | bytes 3763204 | tf_op jit(solution)/shard_map/dynamic_update_slice | solution.py:21
  283.7 5.8 %multiply_convert_fusion = bf16[256,1680]{0,1:T(8,128)(2,1)S(1)} fusion(bf16[256,2240]{1,0:T(8,128)(2,1)} %bitcast.49, bf16[2240,1680]{0,1:T(8,128)(2,1)} %bitcast.45), kind=kOutput, calls=%fused_computation.10 | convolution fusion | flops 1928908800 | bytes 9533440 | tf_op jit(solution)/shard_map/dot_general | solution.py:110
  289.6 0.6 copy.38
  290.2 3.4 collective-permute-start.3
  293.6 1.3 collective-permute-start.4
  295.0 0.1 mul.203
  295.0 0.1 mul.206
  295.1 0.1 mul.209
  295.2 0.1 mul.212
  295.3 0.1 mul.215
  295.4 0.1 mul.218
  295.4 0.1 mul.221
  295.5 0.1 mul.224
  295.6 0.1 mul.227
  295.7 12.1 %collective-permute-done.3 = bf16[4,1,64,1680]{3,2,0,1:T(8,128)(2,1)S(1)} collective-permute-done((bf16[4,1,64,1680]{3,2,0,1:T(8,128)(2,1)S(1)}, bf16[4,1,64,1680]{3,2,0,1:T(8,128)(2,1)S(1)}, u32[]{:S(2)}, u32[]{:S(2)}) %collective-permute-start.3) | collective-permute-done | bytes 860192 | tf_op jit(solution)/shard_map/ppermute | solution.py:38
  307.7 5.5 %collective-permute-done.4 = bf16[4,1,64,1680]{3,2,0,1:T(8,128)(2,1)S(1)} collective-permute-done((bf16[4,1,64,1680]{3,2,0,1:T(8,128)(2,1)S(1)}, bf16[4,1,64,1680]{3,2,0,1:T(8,128)(2,1)S(1)}, u32[]{:S(2)}, u32[]{:S(2)}) %collective-permute-start.4) | collective-permute-done | bytes 860192 | tf_op jit(solution)/shard_map/ppermute | solution.py:40
  313.2 1.1 fusion.5
  314.3 1.8 multiply_add_fusion
  316.1 0.4 fusion.8
  316.5 2.4 convolution_convert_fusion
  318.9 0.0 reduce-scatter.5.cloned.1.call-update
  318.9 24.3 %reduce-scatter.5.cloned.1.call-done = bf16[64,2240]{1,0:T(8,128)(2,1)} async-done(((bf16[256,2240]{1,0:T(8,128)(2,1)}), bf16[64,2240]{1,0:T(8,128)(2,1)}) %reduce-scatter.5.cloned.1.call-update) | async-done | bytes 286736 | tf_op jit(solution)/shard_map/reduce_scatter | solution.py:123
  343.2 1.7 fusion.16
  (26 shorter events, 0.1 us)
Async XLA Ops:
  7.2 111.3 %reduce-scatter.3.cloned.1.call-start = ((), (), s32[]{:S(2)}) async-start(), calls=%async_computation.2 | async-start | bytes 716800 | tf_op jit(solution)/shard_map/reduce_scatter | solution.py:77
  8.7 3.1 copy-start
  11.7 6.7 %copy-start.2 = (bf16[1,1,64,2240]{3,2,1,0:T(8,128)(2,1)S(1)}, bf16[1,1,64,2240]{3,2,1,0:T(8,128)(2,1)}, u32[]{:S(2)}) copy-start(bf16[1,1,64,2240]{3,2,1,0:T(8,128)(2,1)} %param.9) | copy-start | bytes 860164
  11.7 7.1 %copy-start.4 = (bf16[2240]{0:T(1024)(128)(2,1)S(1)}, bf16[2240]{0:T(1024)(128)(2,1)}, u32[]{:S(2)}) copy-start(bf16[2240]{0:T(1024)(128)(2,1)} %param.13) | copy-start | bytes 13444
  11.7 7.2 %copy-start.5 = (bf16[2240]{0:T(1024)(128)(2,1)S(1)}, bf16[2240]{0:T(1024)(128)(2,1)}, u32[]{:S(2)}) copy-start(bf16[2240]{0:T(1024)(128)(2,1)} %param.14) | copy-start | bytes 13444
  11.8 7.2 %copy-start.6 = (u32[32]{0:T(128)S(1)}, u32[32]{0:T(128)}, u32[]{:S(2)}) copy-start(u32[32]{0:T(128)} %constant.64) | copy-start | bytes 388
  11.8 271.9 %all-gather.2.cloned.1.call-start = ((), (), s32[]{:S(2)}) async-start(), calls=%async_computation.3 | async-start | bytes 1474560 | tf_op jit(solution)/shard_map/all_gather | solution.py:107
  13.4 159.0 %collective-permute-start = (bf16[560,2,840]{2,0,1:T(8,128)(2,1)}, bf16[560,2,840]{2,0,1:T(8,128)(2,1)}, u32[]{:S(2)}, u32[]{:S(2)}) collective-permute-start(bf16[560,2,840]{2,0,1:T(8,128)(2,1)} %copy.33), channel_id=1, source_target_pairs={{0,1},{1,2},{2,3},{3,0},{4,5},{5,6},{6,7},{7,4},{8,9},{9,10},{10,1... | collective-permute-start | bytes 5644808 | tf_op jit(solution)/shard_map/ppermute | solution.py:20
  16.4 213.2 %collective-permute-start.1 = (bf16[560,2,840]{2,0,1:T(8,128)(2,1)}, bf16[560,2,840]{2,0,1:T(8,128)(2,1)}, u32[]{:S(2)}, u32[]{:S(2)}) collective-permute-start(bf16[560,2,840]{2,0,1:T(8,128)(2,1)} %copy.33), channel_id=1, source_target_pairs={{0,3},{1,0},{2,1},{3,2},{4,7},{5,4},{6,5},{7,6},{8,11},{9,8},{10,9... | collective-permute-start | bytes 5644808 | tf_op jit(solution)/shard_map/ppermute | solution.py:23
  171.1 1.0 copy-start.1
  172.4 84.3 %collective-permute-start.2 = (bf16[560,2,840]{2,0,1:T(8,128)(2,1)}, bf16[560,2,840]{2,0,1:T(8,128)(2,1)}, u32[]{:S(2)}, u32[]{:S(2)}) collective-permute-start(bf16[560,2,840]{2,0,1:T(8,128)(2,1)} %collective-permute-done), channel_id=1, source_target_pairs={{0,1},{1,2},{2,3},{3,0},{4,5},{5,6},{6,7},{7,4},{8,9},{9,10},{10,1... | collective-permute-start | bytes 5644808 | tf_op jit(solution)/shard_map/ppermute | solution.py:20
  173.6 169.6 %reduce-scatter.5.cloned.1.call-start = ((), (), s32[]{:S(2)}) async-start(), calls=%async_computation.4 | async-start | bytes 1474560 | tf_op jit(solution)/shard_map/reduce_scatter | solution.py:123
  283.7 11.2 %copy-start.3 = (bf16[9,2,840]{2,1,0:T(2,128)(2,1)S(1)}, bf16[9,2,840]{2,1,0:T(2,128)(2,1)}, u32[]{:S(2)}) copy-start(bf16[9,2,840]{2,1,0:T(2,128)(2,1)} %param.16) | copy-start | bytes 90724
  290.2 17.6 %collective-permute-start.3 = (bf16[4,1,64,1680]{3,2,0,1:T(8,128)(2,1)S(1)}, bf16[4,1,64,1680]{3,2,0,1:T(8,128)(2,1)S(1)}, u32[]{:S(2)}, u32[]{:S(2)}) collective-permute-start(bf16[4,1,64,1680]{3,2,0,1:T(8,128)(2,1)S(1)} %bitcast.41), channel_id=1, source_target_pairs={{0,1},{1,2},{2,3},{4,5},{5,6},{6,7},{8,9},{9,10},{10,11},{12,13},{... | collective-permute-start | bytes 2580488 | tf_op jit(solution)/shard_map/ppermute | solution.py:38
  293.6 19.6 %collective-permute-start.4 = (bf16[4,1,64,1680]{3,2,0,1:T(8,128)(2,1)S(1)}, bf16[4,1,64,1680]{3,2,0,1:T(8,128)(2,1)S(1)}, u32[]{:S(2)}, u32[]{:S(2)}) collective-permute-start(bf16[4,1,64,1680]{3,2,0,1:T(8,128)(2,1)S(1)} %bitcast.42), channel_id=1, source_target_pairs={{1,0},{2,1},{3,2},{5,4},{6,5},{7,6},{9,8},{10,9},{11,10},{13,12},{... | collective-permute-start | bytes 2580488 | tf_op jit(solution)/shard_map/ppermute | solution.py:40
  314.3 2.2 copy-start.7
Sparse Core Ops, SparseCore 0:
  11.8 65.7 reduce-scatter.2
  173.7 18.8 all-gather.1
  319.0 24.1 reduce-scatter.4
